TPU v7x, 256 devices: a whole 4x4x8 slice. The times are simulated.
256 devices in a mesh: rep: 8 (over z), shard: 32 (over y, x, core).
Axes of the slice: x: 4, y: 4, z: 8, core: 2. Of those that a mesh axis runs over, the one named last changes fastest.
Arguments:
- grad_joined: bfloat16 [8, 1024, 3072], P('rep', 'shard')
- error_joined: float32 [8, 1024, 3072], P('rep', 'shard'), may hold values from -6 to 6
- moment_joined: float32 [1024, 3072], P('shard'), may hold values from -6 to 6
- weight_joined: float32 [1024, 3072], P('shard'), may hold values from -0.1875 to 0.1875
- factor_joined: float32 [32, 3072], replicated, may hold values from -6 to 6
- grad_dense: bfloat16 [8, 1024, 1024], P('rep', 'shard')
- error_dense: float32 [8, 1024, 1024], P('rep', 'shard'), may hold values from -6 to 6
- moment_dense: float32 [1024, 1024], P('shard'), may hold values from -6 to 6
- weight_dense: float32 [1024, 1024], P('shard'), may hold values from -0.1875 to 0.1875
- factor_dense: float32 [32, 1024], replicated, may hold values from -6 to 6
- grad_expand: bfloat16 [8, 1024, 4096], P('rep', 'shard')
- error_expand: float32 [8, 1024, 4096], P('rep', 'shard'), may hold values from -6 to 6
- moment_expand: float32 [1024, 4096], P('shard'), may hold values from -6 to 6
- weight_expand: float32 [1024, 4096], P('shard'), may hold values from -0.1875 to 0.1875
- factor_expand: float32 [32, 4096], replicated, may hold values from -6 to 6
- grad_shrink: bfloat16 [8, 4096, 1024], P('rep', 'shard')
- error_shrink: float32 [8, 4096, 1024], P('rep', 'shard'), may hold values from -6 to 6
- moment_shrink: float32 [4096, 1024], P('shard'), may hold values from -6 to 6
- weight_shrink: float32 [4096, 1024], P('shard'), may hold values from -0.09375 to 0.09375
- factor_shrink: float32 [32, 1024], replicated, may hold values from -6 to 6
- vector_grad: bfloat16 [8, 13312], P('rep', 'shard'), may hold values from -6 to 6
- vector_moment: float32 [13312], P('shard'), may hold values from -6 to 6
- vector_weight: float32 [13312], P('shard'), may hold values from -1.5 to 1.5
Outputs:
- errors_joined: float32 [8, 1024, 3072], P('rep', 'shard')
- moments_joined: float32 [1024, 3072], P('shard')
- weights_joined: float32 [1024, 3072], P('shard')
- factors_joined: float32 [32, 3072], replicated
- errors_dense: float32 [8, 1024, 1024], P('rep', 'shard')
- moments_dense: float32 [1024, 1024], P('shard')
- weights_dense: float32 [1024, 1024], P('shard')
- factors_dense: float32 [32, 1024], replicated
- errors_expand: float32 [8, 1024, 4096], P('rep', 'shard')
- moments_expand: float32 [1024, 4096], P('shard')
- weights_expand: float32 [1024, 4096], P('shard')
- factors_expand: float32 [32, 4096], replicated
- errors_shrink: float32 [8, 4096, 1024], P('rep', 'shard')
- moments_shrink: float32 [4096, 1024], P('shard')
- weights_shrink: float32 [4096, 1024], P('shard')
- factors_shrink: float32 [32, 1024], replicated
- vector_moments: float32 [13312], P('shard')
- vector_weights: float32 [13312], P('shard')
All inputs are finite; a program needn't handle non-finite values.
Results may differ from a plain program's by a relative error of at most 0.0003.
Values sent between devices are 32-bit elements; how exact they have to be, the bound alone decides.
No kernel may reach another device: no remote copies, remote signals or barrier semaphores. Data moves between devices by JAX's collectives and lax.ppermute only.
A program may use at most 128 MiB of HBM per device.

v0:
```python
import jax
import jax.numpy as jnp
from jax import lax
from jax.sharding import PartitionSpec as P

ROUNDS = 2


HIGHEST_PRECISION = lax.Precision.HIGHEST
momentum_decay = 0.9
learn_rate = 0.1


def row_product(factor, matrix):
    return lax.dot_general(
        factor,
        matrix,
        (((1,), (1,)), ((), ())),
        precision=HIGHEST_PRECISION,
        preferred_element_type=jnp.float32,
    )


def gram_of(row_factor):
    return jnp.dot(row_factor, row_factor.T, precision=HIGHEST_PRECISION)


def orthonormal(row_factor, gram_matrix):
    cholesky_factor = jnp.linalg.cholesky(gram_matrix)
    return jax.scipy.linalg.solve_triangular(cholesky_factor, row_factor, lower=True)


def shards(
    grad_joined,
    error_joined,
    moment_joined,
    weight_joined,
    factor_joined,
    grad_dense,
    error_dense,
    moment_dense,
    weight_dense,
    factor_dense,
    grad_expand,
    error_expand,
    moment_expand,
    weight_expand,
    factor_expand,
    grad_shrink,
    error_shrink,
    moment_shrink,
    weight_shrink,
    factor_shrink,
    vector_grad,
    vector_moment,
    vector_weight,
):
    replicas = lax.axis_size("rep")
    gradients = [grad_joined, grad_dense, grad_expand, grad_shrink]
    carried = [error_joined, error_dense, error_expand, error_shrink]
    moment_list = [moment_joined, moment_dense, moment_expand, moment_shrink]
    weight_list = [weight_joined, weight_dense, weight_expand, weight_shrink]
    factors = [factor_joined, factor_dense, factor_expand, factor_shrink]
    corrected = [
        gradients[member][0].astype(jnp.float32) + carried[member][0] for member in range(4)
    ]
    basis_list = []
    for sweep in range(ROUNDS):
        projected = [row_product(factors[member], corrected[member]) for member in range(4)]
        summed = lax.psum((projected[0], projected[1], projected[2], projected[3]), "rep")
        gram_list = lax.psum(
            (gram_of(summed[0]), gram_of(summed[1]), gram_of(summed[2]), gram_of(summed[3])),
            "shard",
        )
        basis_list = [orthonormal(summed[member], gram_list[member]) for member in range(4)]
        partials = [
            jnp.dot(basis_list[member], corrected[member], precision=HIGHEST_PRECISION)
            for member in range(4)
        ]
        totals = lax.psum((partials[0], partials[1], partials[2], partials[3]), ("rep", "shard"))
        factors = [totals[member] / replicas for member in range(4)]
    results = []
    for member in range(4):
        approx = jnp.dot(basis_list[member].T, factors[member], precision=HIGHEST_PRECISION)
        errors = (corrected[member] - approx)[None]
        moments = momentum_decay * moment_list[member] + approx
        weights = weight_list[member] - learn_rate * moments
        results.extend([errors, moments, weights, factors[member]])
    vector_total = lax.psum(vector_grad[0].astype(jnp.float32), "rep")
    vector_moments = momentum_decay * vector_moment + vector_total / replicas
    vector_weights = vector_weight - learn_rate * vector_moments
    results.extend([vector_moments, vector_weights])
    return tuple(results)


def solution(mesh):
    return jax.shard_map(
        shards,
        mesh=mesh,
        in_specs=(
            P("rep", "shard", None),
            P("rep", "shard", None),
            P("shard", None),
            P("shard", None),
            P(),
            P("rep", "shard", None),
            P("rep", "shard", None),
            P("shard", None),
            P("shard", None),
            P(),
            P("rep", "shard", None),
            P("rep", "shard", None),
            P("shard", None),
            P("shard", None),
            P(),
            P("rep", "shard", None),
            P("rep", "shard", None),
            P("shard", None),
            P("shard", None),
            P(),
            P("rep", "shard"),
            P("shard"),
            P("shard"),
        ),
        out_specs=(
            P("rep", "shard", None),
            P("shard", None),
            P("shard", None),
            P(),
            P("rep", "shard", None),
            P("shard", None),
            P("shard", None),
            P(),
            P("rep", "shard", None),
            P("shard", None),
            P("shard", None),
            P(),
            P("rep", "shard", None),
            P("shard", None),
            P("shard", None),
            P(),
            P("shard"),
            P("shard"),
        ),
        check_vma=False,
    )
```

profile of v0, /device:TPU:2, one launch (start us, length us, event | category | flops | bytes accessed | tf_op | source)
XLA Modules:
  0.0 919.8 jit_solution(10872664302884516997)
XLA Ops:
  11.6 33.4 %all-reduce.5 = (f32[32,32]{0,1:T(8,128)S(1)}, f32[32,32]{0,1:T(8,128)S(1)}, f32[32,32]{0,1:T(8,128)S(1)}, f32[32,128]{1,0:T(8,128)S(1)}) all-reduce(f32[32,32]{0,1:T(8,128)S(1)} %convolution_bitcast_fusion.3, f32[32,32]{0,1:T(8,128)S(1)} %convolution_bitcast_fusion.2, ...), channel_id=1, replica_groups=mesh['rep'=8,'shard'=32] {'rep'}, use_global_device_ids=true, to_apply=%region_0.0 | all-reduce | flops 7168 | bytes 57344 | tf_op jit(solution)/shard_map/psum | solution.py:70
  45.8 119.1 %all-reduce.3 = (f32[32,32]{0,1:T(8,128)S(1)}, f32[32,32]{0,1:T(8,128)S(1)}, f32[32,32]{0,1:T(8,128)S(1)}, f32[32,32]{0,1:T(8,128)S(1)}) all-reduce(f32[32,32]{0,1:T(8,128)S(1)} %fusion.78, f32[32,32]{0,1:T(8,128)S(1)} %fusion.80, f32[32,32]{0,1:T(8,128)S(1)} %fusion.82, ...), channel_id=1, replica_groups=mesh['rep'=8,'shard'=32] {'shard'}, use_global_device_ids=true, to_apply=%region_1.0 | all-reduce | flops 4096 | bytes 32768 | tf_op jit(solution)/shard_map/psum | solution.py:71
  165.0 2.9 cholesky.200
  169.3 2.4 custom-call.20
  173.1 2.9 cholesky.178
  177.3 2.4 custom-call.18
  181.5 2.9 cholesky.156
  185.8 2.4 custom-call.16
  189.4 2.9 cholesky.134
  193.6 2.4 custom-call.14
  198.2 259.8 %all-reduce.11.cloned.1.call-done = (f32[32,3072]{1,0:T(8,128)}, f32[32,1024]{1,0:T(8,128)}, f32[32,4096]{1,0:T(8,128)}, f32[32,1024]{1,0:T(8,128)}) async-done(((f32[32,3072]{1,0:T(8,128)}, f32[32,1024]{1,0:T(8,128)}, f32[32,4096]{1,0:T(8,128)}, f32[32,1024]{1,0:T(8,128)}), (f32[32,3072]{1,0:T(8,128)}, f32[32,1024]{1,0:T(8,128)}, f32[32,4096]{1,0:T(8,128)}, ...) | async-done | bytes 1179664 | tf_op jit(solution)/shard_map/psum | solution.py:80
  461.7 27.9 %all-reduce.4 = (f32[32,32]{1,0:T(8,128)S(1)}, f32[32,32]{1,0:T(8,128)S(1)}, f32[32,32]{1,0:T(8,128)S(1)}, f32[32,128]{1,0:T(8,128)S(1)}, f32[416]{0:T(512)S(1)}) all-reduce(f32[32,32]{1,0:T(8,128)S(1)} %fusion.19, f32[32,32]{1,0:T(8,128)S(1)} %fusion.30, f32[32,32]{1,0:T(8,128)S(1)} %fusion.10, ...), channel_id=1, replica_groups=mesh['rep'=8,'shard'=32] {'rep'}, use_global_device_ids=true, to_apply=%region_5.8 | all-reduce | flops 7584 | bytes 60672 | tf_op jit(solution)/shard_map/psum | solution.py:70
  490.2 119.1 %all-reduce.2 = (f32[32,32]{0,1:T(8,128)S(1)}, f32[32,32]{0,1:T(8,128)S(1)}, f32[32,32]{0,1:T(8,128)S(1)}, f32[32,32]{0,1:T(8,128)S(1)}) all-reduce(f32[32,32]{0,1:T(8,128)S(1)} %fusion.79, f32[32,32]{0,1:T(8,128)S(1)} %fusion.81, f32[32,32]{0,1:T(8,128)S(1)} %fusion.83, ...), channel_id=1, replica_groups=mesh['rep'=8,'shard'=32] {'shard'}, use_global_device_ids=true, to_apply=%region_6.9 | all-reduce | flops 4096 | bytes 32768 | tf_op jit(solution)/shard_map/psum | solution.py:71
  609.5 2.9 cholesky.211
  613.7 2.4 custom-call.21
  617.5 2.9 cholesky.189
  621.8 2.4 custom-call.19
  625.9 2.9 cholesky.167
  630.2 2.4 custom-call.17
  633.8 2.9 cholesky.145
  638.1 2.4 custom-call.15
  643.3 259.6 %all-reduce.9.cloned.1.call-done = (f32[32,3072]{1,0:T(8,128)}, f32[32,1024]{1,0:T(8,128)}, f32[32,4096]{1,0:T(8,128)}, f32[32,1024]{1,0:T(8,128)}) async-done(((f32[32,3072]{1,0:T(8,128)}, f32[32,1024]{1,0:T(8,128)}, f32[32,4096]{1,0:T(8,128)}, f32[32,1024]{1,0:T(8,128)}), (f32[32,3072]{1,0:T(8,128)}, f32[32,1024]{1,0:T(8,128)}, f32[32,4096]{1,0:T(8,128)}, ...) | async-done | bytes 1179664 | tf_op jit(solution)/shard_map/psum | solution.py:80
  906.4 1.9 multiply_subtract_fusion
  908.3 1.9 multiply_subtract_fusion.1
  (144 shorter events, 39.7 us)
Async XLA Ops:
  7.2 1.9 copy-start
  7.2 1.9 copy-start.5
  7.2 1.9 copy-start.2
  7.2 450.7 %all-reduce.11.cloned.1.call-start = ((), (), s32[]{:S(2)}) async-start(), calls=%async_computation.1 | async-start | bytes 2359296 | tf_op jit(solution)/shard_map/psum | solution.py:80
  9.2 1.2 copy-start.3
  9.2 1.2 copy-start.18
  11.1 160.8 %copy-start.4 = (bf16[1,128,1024]{2,1,0:T(8,128)(2,1)S(1)}, bf16[1,128,1024]{2,1,0:T(8,128)(2,1)}, u32[]{:S(2)}) copy-start(bf16[1,128,1024]{2,1,0:T(8,128)(2,1)} %param.43) | copy-start | bytes 786436
  11.6 160.4 %copy-start.1 = (f32[1,128,1024]{2,1,0:T(8,128)S(1)}, f32[1,128,1024]{2,1,0:T(8,128)}, u32[]{:S(2)}) copy-start(f32[1,128,1024]{2,1,0:T(8,128)} %param.44) | copy-start | bytes 1572868
  197.5 705.3 %all-reduce.9.cloned.1.call-start = ((), (), s32[]{:S(2)}) async-start(), calls=%async_computation | async-start | bytes 2359296 | tf_op jit(solution)/shard_map/psum | solution.py:80
  457.9 1.7 copy-start.19
  903.7 1.3 copy-start.11
  903.8 1.2 copy-start.27
  903.8 1.3 copy-start.17
  904.9 3.4 copy-start.8
  905.0 1.3 copy-start.12
  905.0 1.4 copy-start.13
  905.0 5.2 copy-start.16
  906.4 4.9 copy-start.10
  906.4 1.9 copy-start.14
  906.4 1.9 copy-start.15
  908.3 1.9 copy-start.22
  908.3 1.9 copy-start.23
  910.2 1.1 copy-start.20
  910.2 1.1 copy-start.21
  (9 other events, 7.6 us)
Sparse Core Ops, SparseCore 0:
  197.6 260.2 all-reduce.10
  642.1 260.6 all-reduce.8
where the time goes:
time: 920 us
  waiting for transfers between devices  519 us (56%)
  blocking collectives  300 us (33%)
  other arithmetic  56.2 us (6%)
  matrix products  24.9 us (3%)
  between operations  14.6 us (2%)
    psum x2, waiting for transfers between devices, shards(): lax.psum((partials[0], partials[1], partials[2], partials[3]), ('rep', 's...  519 us
    psum x2, blocking collectives, shards(): lax.psum((gram_of(summed[0]), gram_of(summed[1]), gram_of(summed[2]), gra...  238 us
    psum x2, blocking collectives, shards(): lax.psum((projected[0], projected[1], projected[2], projected[3]), 'rep')  61.3 us
    another operation x24, other arithmetic, orthonormal(): cholesky_factor = jnp.linalg.cholesky(gram_matrix)  28.7 us
    another operation x16, other arithmetic, orthonormal(): jax.scipy.linalg.solve_triangular(cholesky_factor, row_factor, lower=True)  24.7 us
  transfers between devices with their start and end apart: 2, of which 2 were waited for; matrix products, arithmetic and copies ran while one was open for 0% of the time, Pallas kernels for 0%

commit v1 on v0

v1 whole, which is shorter than its diff:
```python
import jax
import jax.numpy as jnp
from jax import lax
from jax.sharding import PartitionSpec as P

ROUNDS = 2


HIGHEST_PRECISION = lax.Precision.HIGHEST
momentum_decay = 0.9
learn_rate = 0.1


def row_product(factor, matrix):
    return lax.dot_general(
        factor,
        matrix,
        (((1,), (1,)), ((), ())),
        precision=HIGHEST_PRECISION,
        preferred_element_type=jnp.float32,
    )


def gram_of(row_factor):
    return lax.dot_general(
        row_factor,
        row_factor,
        (((1,), (1,)), ((), ())),
        precision=HIGHEST_PRECISION,
        preferred_element_type=jnp.float32,
    )


def mat(a, b):
    return jnp.dot(a, b, precision=HIGHEST_PRECISION, preferred_element_type=jnp.float32)


def inverse_cholesky(grams):
    lower = jnp.linalg.cholesky(grams)
    eye = jnp.broadcast_to(jnp.eye(grams.shape[-1], dtype=grams.dtype), grams.shape)
    return lax.linalg.triangular_solve(lower, eye, left_side=True, lower=True)


def shards(
    grad_joined,
    error_joined,
    moment_joined,
    weight_joined,
    factor_joined,
    grad_dense,
    error_dense,
    moment_dense,
    weight_dense,
    factor_dense,
    grad_expand,
    error_expand,
    moment_expand,
    weight_expand,
    factor_expand,
    grad_shrink,
    error_shrink,
    moment_shrink,
    weight_shrink,
    factor_shrink,
    vector_grad,
    vector_moment,
    vector_weight,
):
    replicas = lax.axis_size("rep")
    first_replica = lax.axis_index("rep") == 0
    gradients = [grad_joined, grad_dense, grad_expand, grad_shrink]
    carried = [error_joined, error_dense, error_expand, error_shrink]
    moment_list = [moment_joined, moment_dense, moment_expand, moment_shrink]
    weight_list = [weight_joined, weight_dense, weight_expand, weight_shrink]
    factors = [factor_joined, factor_dense, factor_expand, factor_shrink]
    members = range(4)
    corrected = [gradients[m][0].astype(jnp.float32) + carried[m][0] for m in members]
    vector_local = vector_grad[0].astype(jnp.float32)
    vector_total = None
    basis_list = []
    for sweep in range(ROUNDS):
        projected = [row_product(factors[m], corrected[m]) for m in members]
        if sweep == 0:
            summed = lax.psum((*projected, vector_local), "rep")
            vector_total = summed[4]
        else:
            summed = lax.psum(tuple(projected), "rep")
        grams = [
            jnp.where(first_replica, gram_of(summed[m]), jnp.zeros((), jnp.float32))
            for m in members
        ]
        partials = [mat(summed[m], corrected[m]) for m in members]
        packed = lax.psum(jnp.concatenate(partials + grams, axis=1), ("rep", "shard"))
        widths = [p.shape[1] for p in partials] + [g.shape[1] for g in grams]
        offsets = [sum(widths[:i]) for i in range(len(widths))]
        pieces = [packed[:, o : o + w] for o, w in zip(offsets, widths)]
        inverse = inverse_cholesky(jnp.stack(pieces[4:]))
        factors = [mat(inverse[m], pieces[m]) / replicas for m in members]
        basis_list = [mat(inverse[m], summed[m]) for m in members]
    results = []
    for m in members:
        approx = lax.dot_general(
            basis_list[m],
            factors[m],
            (((0,), (0,)), ((), ())),
            precision=HIGHEST_PRECISION,
            preferred_element_type=jnp.float32,
        )
        errors = (corrected[m] - approx)[None]
        moments = momentum_decay * moment_list[m] + approx
        weights = weight_list[m] - learn_rate * moments
        results.extend([errors, moments, weights, factors[m]])
    vector_moments = momentum_decay * vector_moment + vector_total / replicas
    vector_weights = vector_weight - learn_rate * vector_moments
    results.extend([vector_moments, vector_weights])
    return tuple(results)


def solution(mesh):
    big = P("rep", "shard", None)
    rows = P("shard", None)
    member_in = (big, big, rows, rows, P())
    member_out = (big, rows, rows, P())
    return jax.shard_map(
        shards,
        mesh=mesh,
        in_specs=member_in * 4 + (P("rep", "shard"), P("shard"), P("shard")),
        out_specs=member_out * 4 + (P("shard"), P("shard")),
        check_vma=False,
    )
```

time: 920 us -> 729 us (0.79)
  blocking collectives: 300 us -> 62.4 us
  matrix products: 24.9 us -> 51.9 us
  waiting for transfers between devices: 519 us -> 542 us
  other arithmetic: 56.2 us -> 44.3 us
    psum x4 -> x2, blocking collectives: 300 us -> 62.4 us  [the longest x1 33.3 us: shards(): summed = lax.psum((*projected, vector_local), 'rep')]
    dot_general x20 -> x32, matrix products: 17 us -> 42.9 us  [the longest x20 28.3 us: mat(): jnp.dot(a, b, precision=HIGHEST_PRECISION, preferred_element_type=jnp.flo...]
    psum x2, waiting for transfers between devices: 519 us -> 542 us  [shards(): lax.psum(jnp.concatenate(partials + grams, axis=1), ('rep', 'shard'))]
    concatenate x0 -> x4, local copies, waits for them, and re-layouts: none -> 11.3 us  [shards(): jnp.concatenate(partials + grams, axis=1)]
    another operation x40 -> x14, other arithmetic: 53.4 us -> 43.6 us  [the longest x7 23.8 us: inverse_cholesky(): lower = jnp.linalg.cholesky(grams)]
where the time goes in v1:
time: 729 us; the launch traced here: 728 us
  waiting for transfers between devices  542 us (74%)
  blocking collectives  62.4 us (9%)
  matrix products  51.9 us (7%)
  other arithmetic  44.3 us (6%)
  between operations  14.8 us (2%)
  local copies, waits for them, and re-layouts  13.2 us (2%)
    psum x2, waiting for transfers between devices, shards(): lax.psum(jnp.concatenate(partials + grams, axis=1), ('rep', 'shard'))  542 us
    psum x1, blocking collectives, shards(): summed = lax.psum((*projected, vector_local), 'rep')  33.3 us
    psum x1, blocking collectives, shards(): summed = lax.psum(tuple(projected), 'rep')  29.1 us
    dot_general x20, matrix products, mat(): jnp.dot(a, b, precision=HIGHEST_PRECISION, preferred_element_type=jnp.flo...  28.3 us
    another operation x7, other arithmetic, inverse_cholesky(): lower = jnp.linalg.cholesky(grams)  23.8 us
    another operation x5, other arithmetic, inverse_cholesky(): return lax.linalg.triangular_solve(lower, eye, left_side=True, lower=True)  19.9 us
  transfers between devices with their start and end apart: 2, of which 2 were waited for; matrix products, arithmetic and copies ran while one was open for 0% of the time, Pallas kernels for 0%

profile of v1, /device:TPU:2, one launch (start us, length us, event | category | flops | bytes accessed | tf_op | source)
XLA Modules:
  0.0 728.3 jit_solution(14023075009774530606)
XLA Ops:
  7.3 1.9 convolution_bitcast_fusion
  9.2 1.7 convolution_bitcast_fusion.1
  12.1 1.7 convolution_bitcast_fusion.3
  13.8 33.3 %all-reduce.1 = (f32[32,32]{0,1:T(8,128)S(1)}, f32[32,32]{0,1:T(8,128)S(1)}, f32[32,32]{0,1:T(8,128)S(1)}, f32[32,128]{1,0:T(8,128)S(1)}) all-reduce(f32[32,32]{0,1:T(8,128)S(1)} %convolution_bitcast_fusion.3, f32[32,32]{0,1:T(8,128)S(1)} %convolution_bitcast_fusion.2, ...), channel_id=1, replica_groups=mesh['rep'=8,'shard'=32] {'rep'}, use_global_device_ids=true, to_apply=%region_0.0 | all-reduce | flops 7168 | bytes 57344 | tf_op jit(solution)/shard_map/psum | solution.py:84
  47.1 1.7 fusion.20
  52.2 4.0 copy.67
  56.4 271.0 %all-reduce.5.cloned.1.call-done = f32[32,9344]{0,1:T(8,128)} async-done(((f32[32,9344]{0,1:T(8,128)}), f32[32,9344]{0,1:T(8,128)}) %all-reduce.5.cloned.1.call-update) | async-done | bytes 1196048 | tf_op jit(solution)/shard_map/psum | solution.py:93
  328.2 11.7 %custom-call.8 = f32[4,32,32]{2,1,0:T(8,128)S(1)} custom-call(f32[4,32,32]{2,1,0:T(8,128)S(1)} %fusion.45), custom_call_target="Cholesky" | custom-call | tf_op jit(solution)/shard_map/jit(cholesky)/cholesky | solution.py:39
  340.2 9.8 %custom-call.9 = f32[4,1,32,32]{2,3,1,0:T(8,128)S(1)} custom-call(f32[4,1,32,32]{3,2,1,0:T(8,128)S(1)} %select_bitcast_fusion.1), custom_call_target="InvertDiagBlocksLowerTriangular" | custom-call | tf_op jit(solution)/shard_map/triangular_solve/custom-call.0 | solution.py:41
  350.3 1.6 convolution_multiply_fusion.6
  352.6 3.8 convolution_multiply_fusion.1
  357.0 1.6 convolution_multiply_fusion.7
  358.9 3.0 convolution_multiply_fusion.3
  362.5 29.1 %all-reduce = (f32[32,32]{1,0:T(8,128)S(1)}, f32[32,32]{1,0:T(8,128)}, f32[32,32]{1,0:T(8,128)}, f32[32,128]{1,0:T(8,128)S(1)}, f32[416]{0:T(512)}) all-reduce(f32[32,32]{1,0:T(8,128)S(1)} %fusion.26, f32[32,32]{1,0:T(8,128)S(1)} %fusion.34, f32[32,32]{1,0:T(8,128)S(1)} %fusion.18, ...), channel_id=1, replica_groups=mesh['rep'=8,'shard'=32] {'rep'}, use_global_device_ids=true, to_apply=%region_7.0 | all-reduce | flops 7584 | bytes 60672 | tf_op jit(solution)/shard_map/psum | solution.py:87
  400.7 2.1 concatenate.7
  402.9 4.0 copy.70
  407.6 270.8 %all-reduce.7.cloned.1.call-done = f32[32,9344]{0,1:T(8,128)} async-done(((f32[32,9344]{0,1:T(8,128)}), f32[32,9344]{0,1:T(8,128)}) %all-reduce.7.cloned.1.call-update) | async-done | bytes 1196048 | tf_op jit(solution)/shard_map/psum | solution.py:93
  679.2 11.7 %custom-call.10 = f32[4,32,32]{2,1,0:T(8,128)S(1)} custom-call(f32[4,32,32]{2,1,0:T(8,128)S(1)} %fusion.42), custom_call_target="Cholesky" | custom-call | tf_op jit(solution)/shard_map/jit(cholesky)/cholesky | solution.py:39
  691.2 9.8 %custom-call.11 = f32[4,1,32,32]{2,3,1,0:T(8,128)S(1)} custom-call(f32[4,1,32,32]{3,2,1,0:T(8,128)S(1)} %select_bitcast_fusion), custom_call_target="InvertDiagBlocksLowerTriangular" | custom-call | tf_op jit(solution)/shard_map/triangular_solve/custom-call.0 | solution.py:41
  702.0 1.7 convolution_multiply_fusion.4
  703.7 3.2 multiply_subtract_fusion
  706.9 3.8 convolution_multiply_fusion
  710.7 3.3 multiply_subtract_fusion.1
  716.7 3.0 convolution_multiply_fusion.2
  (115 shorter events, 24.3 us)
Async XLA Ops:
  7.2 42.8 %copy-start.4 = (bf16[1,128,1024]{2,1,0:T(8,128)(2,1)S(1)}, bf16[1,128,1024]{2,1,0:T(8,128)(2,1)}, u32[]{:S(2)}) copy-start(bf16[1,128,1024]{2,1,0:T(8,128)(2,1)} %param.41) | copy-start | bytes 786436
  7.2 42.8 %copy-start.1 = (f32[1,128,1024]{2,1,0:T(8,128)S(1)}, f32[1,128,1024]{2,1,0:T(8,128)}, u32[]{:S(2)}) copy-start(f32[1,128,1024]{2,1,0:T(8,128)} %param.42) | copy-start | bytes 1572868
  7.2 43.4 %copy-start.9 = (bf16[1,32,1024]{2,1,0:T(8,128)(2,1)S(1)}, bf16[1,32,1024]{2,1,0:T(8,128)(2,1)}, u32[]{:S(2)}) copy-start(bf16[1,32,1024]{2,1,0:T(8,128)(2,1)} %param.31) | copy-start | bytes 196612
  7.2 43.4 %copy-start.7 = (f32[1,32,1024]{2,1,0:T(8,128)S(1)}, f32[1,32,1024]{2,1,0:T(8,128)}, u32[]{:S(2)}) copy-start(f32[1,32,1024]{2,1,0:T(8,128)} %param.32) | copy-start | bytes 393220
  7.2 42.0 %copy-start.6 = (bf16[1,32,3072]{2,1,0:T(8,128)(2,1)S(1)}, bf16[1,32,3072]{2,1,0:T(8,128)(2,1)}, u32[]{:S(2)}) copy-start(bf16[1,32,3072]{2,1,0:T(8,128)(2,1)} %param.26) | copy-start | bytes 589828
  7.3 42.0 %copy-start.3 = (f32[1,32,3072]{2,1,0:T(8,128)S(1)}, f32[1,32,3072]{2,1,0:T(8,128)}, u32[]{:S(2)}) copy-start(f32[1,32,3072]{2,1,0:T(8,128)} %param.27) | copy-start | bytes 1179652
  7.3 320.0 %all-reduce.5.cloned.1.call-start = ((), (), s32[]{:S(2)}) async-start(), calls=%async_computation | async-start | bytes 9568256 | tf_op jit(solution)/shard_map/psum | solution.py:93
  56.2 300.2 %copy-start.2 = (f32[1,32,4096]{2,1,0:T(8,128)S(1)}, f32[1,32,4096]{2,1,0:T(8,128)}, u32[]{:S(2)}) copy-start(f32[1,32,4096]{2,1,0:T(8,128)} %param.37) | copy-start | bytes 1572868
  56.2 300.2 %copy-start.5 = (bf16[1,32,4096]{2,1,0:T(8,128)(2,1)S(1)}, bf16[1,32,4096]{2,1,0:T(8,128)(2,1)}, u32[]{:S(2)}) copy-start(bf16[1,32,4096]{2,1,0:T(8,128)(2,1)} %param.36) | copy-start | bytes 786436
  56.2 622.1 %all-reduce.7.cloned.1.call-start = ((), (), s32[]{:S(2)}) async-start(), calls=%async_computation.1 | async-start | bytes 9568256 | tf_op jit(solution)/shard_map/psum | solution.py:93
  56.3 302.4 %copy-start.25 = (pred[32,32]{1,0:T(8,128)(4,1)}, pred[32,32]{1,0:T(8,128)(4,1)S(1)}, u32[]{:S(2)}) copy-start(pred[32,32]{1,0:T(8,128)(4,1)S(1)} %iota_compare_fusion.1) | copy-start | bytes 3076
  56.3 302.3 %copy-start.23 = (pred[32,32]{1,0:T(8,128)(4,1)}, pred[32,32]{1,0:T(8,128)(4,1)S(1)}, u32[]{:S(2)}) copy-start(pred[32,32]{1,0:T(8,128)(4,1)S(1)} %iota_compare_fusion) | copy-start | bytes 3076
  56.3 306.1 %copy-start.19 = (f32[32,32]{1,0:T(8,128)}, f32[32,32]{1,0:T(8,128)S(1)}, u32[]{:S(2)}) copy-start(f32[32,32]{1,0:T(8,128)S(1)} %fusion.52) | copy-start | bytes 12292
  402.9 288.1 %copy-start.26 = (pred[32,32]{1,0:T(8,128)(4,1)S(1)}, pred[32,32]{1,0:T(8,128)(4,1)}, u32[]{:S(2)}) copy-start(pred[32,32]{1,0:T(8,128)(4,1)} %copy-done.25) | copy-start | bytes 3076
  402.9 288.3 %copy-start.24 = (pred[32,32]{1,0:T(8,128)(4,1)S(1)}, pred[32,32]{1,0:T(8,128)(4,1)}, u32[]{:S(2)}) copy-start(pred[32,32]{1,0:T(8,128)(4,1)} %copy-done.23) | copy-start | bytes 3076
  402.9 298.2 %copy-start.20 = (f32[32,32]{1,0:T(8,128)S(1)}, f32[32,32]{1,0:T(8,128)}, u32[]{:S(2)}) copy-start(f32[32,32]{1,0:T(8,128)} %copy-done.19) | copy-start | bytes 12292
  402.9 298.5 %copy-start.16 = (f32[32,128]{1,0:T(8,128)S(1)}, f32[32,128]{1,0:T(8,128)}, u32[]{:S(2)}) copy-start(f32[32,128]{1,0:T(8,128)} %copy-done.15) | copy-start | bytes 49156
  402.9 298.6 %copy-start.18 = (f32[32,32]{1,0:T(8,128)S(1)}, f32[32,32]{1,0:T(8,128)}, u32[]{:S(2)}) copy-start(f32[32,32]{1,0:T(8,128)} %get-tuple-element.22) | copy-start | bytes 12292
  402.9 298.8 %copy-start.17 = (f32[32,32]{1,0:T(8,128)S(1)}, f32[32,32]{1,0:T(8,128)}, u32[]{:S(2)}) copy-start(f32[32,32]{1,0:T(8,128)} %get-tuple-element.21) | copy-start | bytes 12292
  703.7 12.0 %copy-start.21 = (f32[32,1024]{1,0:T(8,128)S(1)}, f32[32,1024]{1,0:T(8,128)}, u32[]{:S(2)}) copy-start(f32[32,1024]{1,0:T(8,128)} %param.34) | copy-start | bytes 393220
  703.7 12.0 %copy-start.22 = (f32[32,1024]{1,0:T(8,128)S(1)}, f32[32,1024]{1,0:T(8,128)}, u32[]{:S(2)}) copy-start(f32[32,1024]{1,0:T(8,128)} %param.33) | copy-start | bytes 393220
  706.8 12.9 %copy-start.13 = (f32[32,3072]{1,0:T(8,128)S(1)}, f32[32,3072]{1,0:T(8,128)}, u32[]{:S(2)}) copy-start(f32[32,3072]{1,0:T(8,128)} %param.29) | copy-start | bytes 1179652
  706.9 13.0 %copy-start.14 = (f32[32,3072]{1,0:T(8,128)S(1)}, f32[32,3072]{1,0:T(8,128)}, u32[]{:S(2)}) copy-start(f32[32,3072]{1,0:T(8,128)} %param.28) | copy-start | bytes 1179652
  710.7 10.8 %copy-start.8 = (f32[32,4096]{1,0:T(8,128)}, f32[32,4096]{1,0:T(8,128)S(1)}, u32[]{:S(2)}) copy-start(f32[32,4096]{1,0:T(8,128)S(1)} %convolution_multiply_fusion) | copy-start | bytes 1572868
  (9 other events, 37.4 us)
Sparse Core Ops, SparseCore 0:
  56.3 270.9 all-reduce.4
  407.1 271.2 all-reduce.6
